TPU v7x, 128 devices: a whole 4x4x4 slice. The times are simulated.
128 devices in a mesh: tm: 32 (over x, z, core), feat: 4 (over y).
Axes of the slice: x: 4, y: 4, z: 4, core: 2. Of those that a mesh axis runs over, the one named last changes fastest.
Arguments:
- activations: bfloat16 [81920, 2048], P(('tm', 'feat')), may hold values from -19 to 19
- targets: bfloat16 [81920, 128], P(('tm', 'feat')), may hold values from -8 to 8
- span_of: int32 [81920], P(('tm', 'feat')), may hold values from 0 to 31, as said below
Outputs:
- predictions: bfloat16 [81920, 128], P(('tm', 'feat'))
- surprise: float32 [81920], P(('tm', 'feat'))
Inputs may be any that keep to these rules, and one draw needn't show every extreme that they name: `span_of`: in each aligned block of 640 rows (the rows of one device) every span from 0 to 31 appears exactly 20 times.
All inputs are finite; a program needn't handle non-finite values.
Results may differ from a plain program's by a relative error of at most 0.0049.
Values may be sent and summed in bfloat16 or wider, within the bound.
No kernel may reach another device: no remote copies, remote signals or barrier semaphores. Data moves between devices by JAX's collectives and lax.ppermute only.
A program may use at most 320 MiB of HBM per device.

v0:
```python
import jax
import jax.numpy as jnp
from jax import lax
from jax.sharding import PartitionSpec as P

ITERS = 3
RIDGE = 0.1
TINY = 1e-06


def carried_in(shard, axis, combine, identity):
    length, position = (lax.axis_size(axis), lax.axis_index(axis))
    everything = jax.tree.map(lambda part: lax.all_gather(part, axis), shard)
    start = jax.tree.map(
        lambda part, zero: jnp.broadcast_to(jnp.asarray(zero, part.dtype), part.shape),
        shard,
        identity,
    )

    def hop(k, before):
        reached = k < position
        new = combine(before, jax.tree.map(lambda part: part[k], everything))
        return jax.tree.map(lambda a, b: jnp.where(reached, a, b), new, before)

    return lax.fori_loop(0, length, hop, start)


def body(activations, targets, span_of):
    spans = lax.axis_size("tm")
    feat_count = lax.axis_size("feat")
    tok_dev, width = activations.shape
    n_targets = targets.shape[1]
    block_rows = width // feat_count
    share = tok_dev // spans
    contract = (((0,), (0,)), ((), ()))
    highest = lax.Precision.HIGHEST
    order = jnp.argsort(span_of, stable=True)
    sorted_x = jnp.take(activations, order, axis=0).reshape(spans, share, width)
    sorted_y = jnp.take(targets, order, axis=0).reshape(spans, share, n_targets)
    moved_x, moved_y = (
        lax.all_to_all(sorted_x, "tm", split_axis=0, concat_axis=0, tiled=True),
        lax.all_to_all(sorted_y, "tm", split_axis=0, concat_axis=0, tiled=True),
    )
    local_x = moved_x.reshape(tok_dev, width)
    local_y = moved_y.reshape(tok_dev, n_targets)
    col_start = lax.axis_index("feat") * block_rows
    rows_x = lax.all_gather(local_x, "feat", axis=0, tiled=True)
    rows_y = lax.all_gather(local_y, "feat", axis=0, tiled=True)
    own = lax.dynamic_slice_in_dim(rows_x, col_start, block_rows, 1)
    gram_part = lax.dot_general(own, rows_x, contract, preferred_element_type=jnp.float32)
    cross_part = lax.dot_general(own, rows_y, contract, preferred_element_type=jnp.float32)

    def combine(earlier, later):
        return (earlier[0] + later[0], earlier[1] + later[1])

    identity = (jnp.zeros_like(gram_part), jnp.zeros_like(cross_part))
    gram_prefix, cross_prefix = carried_in((gram_part, cross_part), "tm", combine, identity)
    seen = (lax.axis_index("tm") * (tok_dev * feat_count)).astype(jnp.float32)
    scale = 1.0 / jnp.maximum(seen, 1.0)
    rhs = scale * cross_prefix

    def column_dot(left, right):
        return lax.psum(jnp.sum(left * right, axis=0), "feat")

    residual = rhs
    direction = rhs
    norm_now = column_dot(residual, residual)
    solution = None
    for step in range(ITERS):
        product = jnp.dot(
            gram_prefix,
            lax.all_gather(direction, "feat", axis=0, tiled=True),
            precision=highest,
            preferred_element_type=jnp.float32,
        )
        product, carried = (product, direction)
        image = scale * product + RIDGE * direction
        alpha = norm_now / (column_dot(direction, image) + TINY)
        update = alpha * carried
        solution = update if solution is None else solution + update
        if step + 1 < ITERS:
            residual = residual - alpha * image
            norm_next = column_dot(residual, residual)
            direction = residual + norm_next / (norm_now + TINY) * direction
            norm_now = norm_next
    weights = lax.all_gather(solution.astype(jnp.bfloat16), "feat", axis=0, tiled=True)
    predicted = jnp.dot(local_x, weights, preferred_element_type=jnp.float32).astype(jnp.bfloat16)
    returned = lax.all_to_all(
        predicted.reshape(spans, share, n_targets), "tm", split_axis=0, concat_axis=0, tiled=True
    )
    in_order = returned.reshape(tok_dev, n_targets)
    predictions = jnp.zeros_like(in_order).at[order].set(in_order)
    error = targets.astype(jnp.float32) - predictions.astype(jnp.float32)
    surprise = jnp.mean(error * error, axis=1)
    return (predictions, surprise)


def solution(mesh):
    return jax.shard_map(
        body,
        mesh=mesh,
        in_specs=(P(("tm", "feat"), None), P(("tm", "feat"), None), P(("tm", "feat"))),
        out_specs=(P(("tm", "feat"), None), P(("tm", "feat"))),
        check_vma=False,
    )
```

profile of v0, /device:TPU:1, one launch (start us, length us, event | category | flops | bytes accessed | tf_op | source)
XLA Modules:
  0.0 1049.8 jit_solution(8673995626986290233)
XLA Ops:
  7.2 5.2 sort.17
  12.5 4.1 gather_fusion
  16.6 5.2 gather.13
  21.9 2.2 broadcast_select_fusion
  24.1 48.7 %all_to_all.15 = bf16[32,20,2048]{2,1,0:T(8,128)(2,1)} all-to-all(bf16[32,20,2048]{2,1,0:T(8,128)(2,1)S(1)} %broadcast_select_fusion), channel_id=1, replica_groups=mesh['tm'=32,'feat'=4] {'tm'}, dimensions={0} | all-to-all | bytes 5242880 | tf_op jit(solution)/shard_map/all_to_all | solution.py:41
  72.8 5.2 reshape.39
  78.1 2.0 gather_fusion.1
  81.0 3.9 all-to-all-start.1
  85.0 8.2 all-to-all-done.1
  93.9 16.8 %all_gather.33 = bf16[2560,128]{1,0:T(8,128)(2,1)S(1)} all-gather(bf16[640,128]{1,0:T(8,128)(2,1)} %reshape.40), channel_id=1, replica_groups=mesh['tm'=32,'feat'=4] {'feat'}, dimensions={0}, use_global_device_ids=true | all-gather | bytes 819200 | tf_op jit(solution)/shard_map/all_gather | solution.py:48
  110.7 71.1 %all-gather.9.cloned.1.call-done = bf16[2560,2048]{1,0:T(8,128)(2,1)} async-done(((bf16[640,2048]{1,0:T(8,128)(2,1)}), bf16[2560,2048]{1,0:T(8,128)(2,1)}) %all-gather.9.cloned.1.call-update) | async-done | bytes 10485776 | tf_op jit(solution)/shard_map/all_gather | solution.py:47
  181.8 3.3 fusion
  185.2 10.5 fusion.2
  195.8 43.9 %all-gather.19.cloned.1.call-done = f32[16384,128]{1,0:T(8,128)} async-done(((f32[512,128]{1,0:T(8,128)}), f32[16384,128]{1,0:T(8,128)}) %all-gather.19.cloned.1.call-update) | async-done | bytes 8388624 | tf_op jit(solution)/shard_map/all_gather | solution.py:13
  239.7 377.4 %all-gather.17.cloned.1.call-done = f32[16384,2048]{1,0:T(8,128)} async-done(((f32[512,2048]{1,0:T(8,128)}), f32[16384,2048]{1,0:T(8,128)}) %all-gather.17.cloned.1.call-update) | async-done | bytes 134217744 | tf_op jit(solution)/shard_map/all_gather | solution.py:13
  617.2 248.0 %while.16 = (s32[]{:T(128)}, f32[512,2048]{1,0:T(8,128)}, f32[512,128]{1,0:T(8,128)S(1)}, s32[]{:T(128)}, f32[32,512,2048]{2,1,0:T(8,128)}, /*index=5*/f32[32,512,128]{2,1,0:T(8,128)}, s32[]{:T(128)}, s32[]{:T(128)}) while((s32[]{:T(128)}, f32[512,2048]{1,0:T(8,128)}, f32[512,128]{1,0:T(8,128)S(1)}, s32[]{:T(128)}, ...), condition=%wide.region_2.3_spmd.clone, body=%wide.region_1.2_spmd.clone.sunk | while | flops 3342340 | bytes 13369459 | solution.py:25
  617.2 5.5 add_select_fusion.4
  623.7 6.7 add_select_fusion.4
  631.5 6.7 add_select_fusion.4
  639.2 6.7 add_select_fusion.4
  647.0 6.7 add_select_fusion.4
  654.8 6.7 add_select_fusion.4
  662.6 6.7 add_select_fusion.4
  670.4 6.7 add_select_fusion.4
  678.2 6.7 add_select_fusion.4
  686.0 6.7 add_select_fusion.4
  693.8 6.7 add_select_fusion.4
  701.6 6.7 add_select_fusion.4
  709.4 6.7 add_select_fusion.4
  717.1 6.7 add_select_fusion.4
  724.9 6.7 add_select_fusion.4
  732.7 6.7 add_select_fusion.4
  740.5 6.7 add_select_fusion.4
  748.3 6.7 add_select_fusion.4
  756.1 6.7 add_select_fusion.4
  763.9 6.7 add_select_fusion.4
  771.7 6.7 add_select_fusion.4
  779.5 6.7 add_select_fusion.4
  787.3 6.7 add_select_fusion.4
  795.0 6.7 add_select_fusion.4
  802.8 6.7 add_select_fusion.4
  810.6 6.7 add_select_fusion.4
  818.4 6.7 add_select_fusion.4
  826.2 6.7 add_select_fusion.4
  834.0 6.7 add_select_fusion.4
  841.8 6.7 add_select_fusion.4
  849.6 6.7 add_select_fusion.4
  857.4 6.7 add_select_fusion.4
  866.0 20.6 %all-gather.11.cloned.1.call-done = f32[2048,128]{1,0:T(8,128)} async-done(((f32[512,128]{1,0:T(8,128)}), f32[2048,128]{1,0:T(8,128)}) %all-gather.11.cloned.1.call-update) | async-done | bytes 1048592 | tf_op jit(solution)/shard_map/all_gather | solution.py:72
  886.6 6.6 multiply_reduce_fusion.4
  893.2 7.8 all-reduce
  902.1 6.0 psum.44
  908.9 27.8 %all-gather.13.cloned.1.call-done = f32[2048,128]{1,0:T(8,128)} async-done(((f32[512,128]{1,0:T(8,128)}), f32[2048,128]{1,0:T(8,128)}) %all-gather.13.cloned.1.call-update) | async-done | bytes 1048592 | tf_op jit(solution)/shard_map/all_gather | solution.py:72
  936.7 6.6 multiply_reduce_fusion.2
  943.4 7.7 psum.45
  952.1 6.0 psum.46
  958.2 1.8 multiply_add_fusion
  960.0 27.8 %all-gather.15.cloned.1.call-done = f32[2048,128]{1,0:T(8,128)} async-done(((f32[512,128]{1,0:T(8,128)}), f32[2048,128]{1,0:T(8,128)}) %all-gather.15.cloned.1.call-update) | async-done | bytes 1048592 | tf_op jit(solution)/shard_map/all_gather | solution.py:72
  987.8 5.9 fusion.8
  993.7 7.7 psum.47
  1002.5 10.6 %all_gather.39 = bf16[2048,128]{1,0:T(8,128)(2,1)S(1)} all-gather(bf16[512,128]{1,0:T(8,128)(2,1)S(1)} %add_convert_fusion), channel_id=1, replica_groups=mesh['tm'=32,'feat'=4] {'feat'}, dimensions={0}, use_global_device_ids=true | all-gather | bytes 655360 | tf_op jit(solution)/shard_map/all_gather | solution.py:86
  1013.1 2.6 convolution_convert_fusion
  1015.7 22.1 %all_to_all.16 = bf16[32,20,128]{2,1,0:T(8,128)(2,1)S(1)} all-to-all(bf16[32,20,128]{2,1,0:T(8,128)(2,1)S(1)} %reshape.41), channel_id=1, replica_groups=mesh['tm'=32,'feat'=4] {'tm'}, dimensions={0} | all-to-all | bytes 327680 | tf_op jit(solution)/shard_map/all_to_all | solution.py:88
  1037.9 4.3 scatter_custom_fusion
  (78 shorter events, 40.3 us)
Async XLA Ops:
  7.2 5.3 copy-start
  7.2 174.6 %all-gather.9.cloned.1.call-start = ((), (), s32[]{:S(2)}) async-start(), calls=%async_computation.3 | async-start | bytes 13107200 | tf_op jit(solution)/shard_map/all_gather | solution.py:47
  72.8 5.3 copy-start.1
  81.0 12.2 %all-to-all-start.1 = ((bf16[32,20,128]{2,1,0:T(8,128)(2,1)}), bf16[32,20,128]{2,1,0:T(8,128)(2,1)S(1)}, u32[]{:S(2)}, u32[]{:S(2)}) async-start(bf16[32,20,128]{2,1,0:T(8,128)(2,1)} %broadcast_select_fusion.1), calls=%async_computation.1 | async-start | bytes 393216 | tf_op jit(solution)/shard_map/all_to_all | solution.py:42
  84.9 154.8 %all-gather.19.cloned.1.call-start = ((), (), s32[]{:S(2)}) async-start(), calls=%async_computation.8 | async-start | bytes 8650752 | tf_op jit(solution)/shard_map/all_gather | solution.py:13
  185.2 432.0 %all-gather.17.cloned.1.call-start = ((), (), s32[]{:S(2)}) async-start(), calls=%async_computation.7 | async-start | bytes 138412032 | tf_op jit(solution)/shard_map/all_gather | solution.py:13
  195.7 690.9 %all-gather.11.cloned.1.call-start = ((), (), s32[]{:S(2)}) async-start(), calls=%async_computation.4 | async-start | bytes 1310720 | tf_op jit(solution)/shard_map/all_gather | solution.py:72
  865.9 70.8 %all-gather.13.cloned.1.call-start = ((), (), s32[]{:S(2)}) async-start(), calls=%async_computation.5 | async-start | bytes 1310720 | tf_op jit(solution)/shard_map/all_gather | solution.py:72
  902.1 6.0 copy-start.3
  908.9 49.3 %copy-start.2 = (f32[512,128]{1,0:T(8,128)S(1)}, f32[512,128]{1,0:T(8,128)}, u32[]{:S(2)}) copy-start(f32[512,128]{1,0:T(8,128)} %multiply_add_fusion.1) | copy-start | bytes 786436
  908.9 78.9 %all-gather.15.cloned.1.call-start = ((), (), s32[]{:S(2)}) async-start(), calls=%async_computation.6 | async-start | bytes 1310720 | tf_op jit(solution)/shard_map/all_gather | solution.py:72
  1042.2 0.8 copy-start.4
Sparse Core Ops, SparseCore 0:
  78.2 103.5 all-gather.8
  185.3 54.3 all-gather.18
  242.0 375.1 all-gather.16
  866.0 20.4 all-gather.10
  909.0 27.6 all-gather.12
  960.1 27.6 all-gather.14
where the time goes:
time: 1050 us
  waiting for transfers between devices  577 us (55%)
  other arithmetic  263 us (25%)
  blocking collectives  133 us (13%)
  matrix products  35.6 us (3%)
  local copies, waits for them, and re-layouts  21.7 us (2%)
  between operations  14.3 us (1%)
    all_gather x2, waiting for transfers between devices, carried_in(): everything = jax.tree.map(lambda part: lax.all_gather(part, axis), shard)  421 us
    select_n x64, other arithmetic, hop(): return jax.tree.map(lambda a, b: jnp.where(reached, a, b), new, before)  247 us
    all_gather x3, waiting for transfers between devices, body(): lax.all_gather(direction, 'feat', axis=0, tiled=True)  76.2 us
    all_gather x1, waiting for transfers between devices, body(): rows_x = lax.all_gather(local_x, 'feat', axis=0, tiled=True)  71.1 us
    all_to_all x1, blocking collectives, body(): lax.all_to_all(sorted_x, 'tm', split_axis=0, concat_axis=0, tiled=True)  48.7 us
    psum x5, blocking collectives, column_dot(): return lax.psum(jnp.sum(left * right, axis=0), 'feat')  35.2 us
    all_to_all x1, blocking collectives, body(): lax.all_to_all(predicted.reshape(spans, share, n_targets), 'tm', split_ax...  22.1 us
  transfers between devices with their start and end apart: 7, of which 7 were waited for; matrix products, arithmetic and copies ran while one was open for 1% of the time, Pallas kernels for 0%

commit v1 on v0

--- a/solution.py
+++ b/solution.py
@@ -6,6 +6,33 @@
 ITERS = 3
 RIDGE = 0.1
 TINY = 1e-06
+
+
+def arrange_figure(array_here, ndim_at):
+    mixed_arr = list(array_here.shape[1:])
+    mixed_arr[ndim_at] *= array_here.shape[0]
+    inter = jnp.moveaxis(array_here, 0, ndim_at).reshape(mixed_arr)
+    return inter
+
+
+def _turn_groups(block_in, chip_axis, array_dim=0):
+    total_devices = lax.psum(1, chip_axis)
+    pool = [(q, (q + 1) % total_devices) for q in range(total_devices)]
+    nodes = [(jj, h) for h, jj in pool]
+    block_now, plain = ([], [])
+    for dev in range(total_devices - 1):
+        if dev % 2 == 0:
+            block_now.append(
+                lax.ppermute(block_now[-1] if block_now else block_in, chip_axis, pool)
+            )
+        else:
+            plain.append(lax.ppermute(plain[-1] if plain else block_in, chip_axis, nodes))
+    v1 = jnp.stack([*block_now[::-1], block_in, *plain], 0)
+    vec_out = lax.axis_index(chip_axis)
+    mid_arr = vec_out - len(block_now)
+    v1 = v1[(jnp.arange(total_devices) - mid_arr) % total_devices]
+    placed = arrange_figure(v1, array_dim)
+    return placed
 
 
 def carried_in(shard, axis, combine, identity):
@@ -69,7 +96,7 @@
     for step in range(ITERS):
         product = jnp.dot(
             gram_prefix,
-            lax.all_gather(direction, "feat", axis=0, tiled=True),
+            _turn_groups(direction, "feat"),
             precision=highest,
             preferred_element_type=jnp.float32,
         )

time: 1050 us -> 1040 us (level)
  waiting for transfers between devices: 577 us -> 538 us
    all_gather x3 -> x0, waiting for transfers between devices: 76.2 us -> none  [body(): lax.all_gather(direction, 'feat', axis=0, tiled=True)]
    ppermute x0 -> x9, waiting for transfers between devices: none -> 37.3 us  [the longest x6 37.3 us: _turn_groups(): lax.ppermute(block_now[-1] if block_now else block_in, chip_axis, pool)]
  transfers between devices with their start and end apart: 7 -> 13, of which waited for: 7 -> 10; matrix products, arithmetic and copies ran while one was open for 1% -> 1% of each run, Pallas kernels for 0% -> 0%
where the time goes in v1:
time: 1040 us
  waiting for transfers between devices  538 us (52%)
  other arithmetic  266 us (26%)
  blocking collectives  140 us (13%)
  matrix products  34.5 us (3%)
  local copies, waits for them, and re-layouts  30.2 us (3%)
  between operations  14 us (1%)
  starting transfers between devices  12.5 us (1%)
    all_gather x2, waiting for transfers between devices, carried_in(): everything = jax.tree.map(lambda part: lax.all_gather(part, axis), shard)  421 us
    select_n x64, other arithmetic, hop(): return jax.tree.map(lambda a, b: jnp.where(reached, a, b), new, before)  247 us
    all_gather x1, waiting for transfers between devices, body(): rows_x = lax.all_gather(local_x, 'feat', axis=0, tiled=True)  71.1 us
    all_to_all x1, blocking collectives, body(): lax.all_to_all(sorted_x, 'tm', split_axis=0, concat_axis=0, tiled=True)  48.7 us
    ppermute x6, waiting for transfers between devices, _turn_groups(): lax.ppermute(block_now[-1] if block_now else block_in, chip_axis, pool)  37.3 us
    psum x5, blocking collectives, column_dot(): return lax.psum(jnp.sum(left * right, axis=0), 'feat')  33.1 us
    all_to_all x1, blocking collectives, body(): lax.all_to_all(predicted.reshape(spans, share, n_targets), 'tm', split_ax...  31.7 us
  transfers between devices with their start and end apart: 13, of which 10 were waited for; matrix products, arithmetic and copies ran while one was open for 1% of the time, Pallas kernels for 0%

profile of v1, /device:TPU:1, one launch (start us, length us, event | category | flops | bytes accessed | tf_op | source)
XLA Modules:
  0.0 1035.9 jit_solution(3006205834173817658)
XLA Ops:
  7.2 5.2 sort.17
  12.5 4.1 gather_fusion
  16.6 5.2 gather.22
  24.1 48.7 %all_to_all.15 = bf16[32,20,2048]{2,1,0:T(8,128)(2,1)} all-to-all(bf16[32,20,2048]{2,1,0:T(8,128)(2,1)S(1)} %broadcast_select_fusion), channel_id=1, replica_groups=mesh['tm'=32,'feat'=4] {'tm'}, dimensions={0} | all-to-all | bytes 5242880 | tf_op jit(solution)/shard_map/all_to_all | solution.py:68
  72.8 5.2 reshape.97
  81.0 3.9 all-to-all-start.1
  85.0 8.2 all-to-all-done.1
  93.9 16.8 %all_gather.24 = bf16[2560,128]{1,0:T(8,128)(2,1)S(1)} all-gather(bf16[640,128]{1,0:T(8,128)(2,1)} %reshape.98), channel_id=1, replica_groups=mesh['tm'=32,'feat'=4] {'feat'}, dimensions={0}, use_global_device_ids=true | all-gather | bytes 819200 | tf_op jit(solution)/shard_map/all_gather | solution.py:75
  110.7 71.1 %all-gather.6.cloned.1.call-done = bf16[2560,2048]{1,0:T(8,128)(2,1)} async-done(((bf16[640,2048]{1,0:T(8,128)(2,1)}), bf16[2560,2048]{1,0:T(8,128)(2,1)}) %all-gather.6.cloned.1.call-update) | async-done | bytes 10485776 | tf_op jit(solution)/shard_map/all_gather | solution.py:74
  181.8 3.3 fusion
  185.2 10.5 %fusion.2 = f32[512,2048]{1,0:T(8,128)} fusion(bf16[2560,2048]{1,0:T(8,128)(2,1)} %all-gather.6.cloned.1.call-done, s32[]{:T(128)S(6)} %select_n.91), kind=kOutput, calls=%fused_computation.11 | convolution fusion | flops 5368709120 | bytes 17301508 | tf_op jit(solution)/shard_map/dot_general | solution.py:77
  195.8 43.9 %all-gather.10.cloned.1.call-done = f32[16384,128]{1,0:T(8,128)} async-done(((f32[512,128]{1,0:T(8,128)}), f32[16384,128]{1,0:T(8,128)}) %all-gather.10.cloned.1.call-update) | async-done | bytes 8388624 | tf_op jit(solution)/shard_map/all_gather | solution.py:40
  239.7 377.4 %all-gather.8.cloned.1.call-done = f32[16384,2048]{1,0:T(8,128)} async-done(((f32[512,2048]{1,0:T(8,128)}), f32[16384,2048]{1,0:T(8,128)}) %all-gather.8.cloned.1.call-update) | async-done | bytes 134217744 | tf_op jit(solution)/shard_map/all_gather | solution.py:40
  617.2 248.0 %while.16 = (s32[]{:T(128)}, f32[512,2048]{1,0:T(8,128)}, f32[512,128]{1,0:T(8,128)S(1)}, s32[]{:T(128)}, f32[32,512,2048]{2,1,0:T(8,128)}, /*index=5*/f32[32,512,128]{2,1,0:T(8,128)}, s32[]{:T(128)}, s32[]{:T(128)}) while((s32[]{:T(128)}, f32[512,2048]{1,0:T(8,128)}, f32[512,128]{1,0:T(8,128)S(1)}, s32[]{:T(128)}, ...), condition=%wide.region_2.3_spmd.clone, body=%wide.region_1.2_spmd.clone.sunk | while | flops 3342340 | bytes 13369459 | solution.py:52
  617.2 5.5 add_select_fusion.4
  623.7 6.7 add_select_fusion.4
  631.5 6.7 add_select_fusion.4
  639.2 6.7 add_select_fusion.4
  647.0 6.7 add_select_fusion.4
  654.8 6.7 add_select_fusion.4
  662.6 6.7 add_select_fusion.4
  670.4 6.7 add_select_fusion.4
  678.2 6.7 add_select_fusion.4
  686.0 6.7 add_select_fusion.4
  693.8 6.7 add_select_fusion.4
  701.6 6.7 add_select_fusion.4
  709.4 6.7 add_select_fusion.4
  717.1 6.7 add_select_fusion.4
  724.9 6.7 add_select_fusion.4
  732.7 6.7 add_select_fusion.4
  740.5 6.7 add_select_fusion.4
  748.3 6.7 add_select_fusion.4
  756.1 6.7 add_select_fusion.4
  763.9 6.7 add_select_fusion.4
  771.7 6.7 add_select_fusion.4
  779.5 6.7 add_select_fusion.4
  787.3 6.7 add_select_fusion.4
  795.0 6.7 add_select_fusion.4
  802.8 6.7 add_select_fusion.4
  810.6 6.7 add_select_fusion.4
  818.4 6.7 add_select_fusion.4
  826.2 6.7 add_select_fusion.4
  834.0 6.7 add_select_fusion.4
  841.8 6.7 add_select_fusion.4
  849.6 6.7 add_select_fusion.4
  857.4 6.7 add_select_fusion.4
  868.0 6.2 collective-permute-done
  874.2 8.1 collective-permute-done.1
  884.3 2.9 gather_fusion.2
  887.2 5.5 multiply_reduce_fusion.4
  892.7 6.0 all-reduce
  899.5 7.7 psum.44
  911.1 3.8 collective-permute-done.3
  915.0 9.0 collective-permute-done.4
  927.9 6.6 multiply_reduce_fusion.2
  934.5 6.0 psum.45
  941.6 7.4 psum.46
  952.9 3.8 collective-permute-done.6
  956.7 6.5 collective-permute-done.7
  967.1 6.0 fusion.8
  973.0 6.0 psum.47
  980.1 9.9 all_gather.27
  992.6 31.7 %all_to_all.16 = bf16[32,20,128]{2,1,0:T(8,128)(2,1)S(1)} all-to-all(bf16[32,20,128]{2,1,0:T(8,128)(2,1)S(1)} %reshape.102), channel_id=1, replica_groups=mesh['tm'=32,'feat'=4] {'tm'}, dimensions={0} | all-to-all | bytes 327680 | tf_op jit(solution)/shard_map/all_to_all | solution.py:115
  1024.3 4.3 scatter_custom_fusion
  (94 shorter events, 65.7 us)
Async XLA Ops:
  7.2 5.3 copy-start
  7.2 174.6 %all-gather.6.cloned.1.call-start = ((), (), s32[]{:S(2)}) async-start(), calls=%async_computation.3 | async-start | bytes 13107200 | tf_op jit(solution)/shard_map/all_gather | solution.py:74
  72.8 5.3 copy-start.1
  81.0 12.2 %all-to-all-start.1 = ((bf16[32,20,128]{2,1,0:T(8,128)(2,1)}), bf16[32,20,128]{2,1,0:T(8,128)(2,1)S(1)}, u32[]{:S(2)}, u32[]{:S(2)}) async-start(bf16[32,20,128]{2,1,0:T(8,128)(2,1)} %broadcast_select_fusion.1), calls=%async_computation.1 | async-start | bytes 393216 | tf_op jit(solution)/shard_map/all_to_all | solution.py:69
  84.9 154.8 %all-gather.10.cloned.1.call-start = ((), (), s32[]{:S(2)}) async-start(), calls=%async_computation.5 | async-start | bytes 8650752 | tf_op jit(solution)/shard_map/all_gather | solution.py:40
  185.2 432.0 %all-gather.8.cloned.1.call-start = ((), (), s32[]{:S(2)}) async-start(), calls=%async_computation.4 | async-start | bytes 138412032 | tf_op jit(solution)/shard_map/all_gather | solution.py:40
  865.2 9.0 collective-permute-start
  866.5 7.7 collective-permute-start.2
  874.2 8.2 collective-permute-start.1
  908.2 6.7 collective-permute-start.3
  908.5 6.5 collective-permute-start.5
  914.9 9.0 collective-permute-start.4
  950.2 13.0 %copy-start.2 = (f32[512,128]{1,0:T(8,128)}, f32[512,128]{1,0:T(8,128)S(1)}, u32[]{:S(2)}) copy-start(f32[512,128]{1,0:T(8,128)S(1)} %multiply_add_fusion) | copy-start | bytes 786436
  950.2 6.5 collective-permute-start.6
  950.3 6.4 collective-permute-start.8
  956.7 6.5 collective-permute-start.7
  1028.6 0.8 copy-start.3
Sparse Core Ops, SparseCore 0:
  78.2 103.5 all-gather.5
  185.3 54.3 all-gather.9
  242.0 375.1 all-gather.7
